TPU v7x, 32 devices: a whole 2x2x4 slice. The times are simulated.
32 devices in a mesh: groups: 2 (over x), dp: 16 (over z, y, core).
Axes of the slice: x: 2, y: 2, z: 4, core: 2. Of those that a mesh axis runs over, the one named last changes fastest.
Arguments:
- frames: bfloat16 [128, 256, 1536], P(('groups', 'dp')), parts along dimension 0, may hold values from -6 to 6
- cotangent: bfloat16 [128, 256, 1536], P(('groups', 'dp')), parts along dimension 0, may hold values from -6 to 6
- gain: float32 [1536], replicated, may hold values from 0.25 to 1.75
- down_weight: bfloat16 [320, 1536, 256], P('groups', 'dp'), parts along dimension 0, may hold values from -0.15625 to 0.15625
- up_weight: bfloat16 [320, 1536, 256], P('groups', 'dp'), parts along dimension 0, may hold values from -0.375 to 0.375
- slot_lang: int32 [32, 2], P('groups'), parts along dimension 0, may hold values from 0 to 159
- utt_slot: int32 [128], P('groups'), parts along dimension 0, may hold values from 0 to 1
- lengths: int32 [128], P('groups'), parts along dimension 0, may hold values from 64 to 256
Outputs:
- frame_grads: bfloat16 [128, 256, 1536], P(('groups', 'dp')), parts along dimension 0
- down_grads: bfloat16 [320, 1536, 256], P('groups', 'dp'), parts along dimension 0
- up_grads: bfloat16 [320, 1536, 256], P('groups', 'dp'), parts along dimension 0
There are 2 independent parts, one for each index of `groups`. A program takes and returns all parts, laid end to end along the dimension named above; an argument that names none is the same for every part. Nothing has to cross between parts.
All inputs are finite; a program needn't handle non-finite values.
Results may differ from a plain program's by a relative error of at most 0.0061.
Values may be sent and summed in bfloat16 or wider, within the bound.
No kernel may reach another device: no remote copies, remote signals or barrier semaphores. Data moves between devices by JAX's collectives and lax.ppermute only.
A program may use at most 128 MiB of HBM per device.

v0:
```python
import jax
import jax.numpy as jnp
from jax import lax
from jax.sharding import PartitionSpec as P


def local_pass(frames, cotangent, gain, w_down, w_up, live_mask, slot_select):
    values = frames.astype(jnp.float32)
    centre_mean = jnp.mean(values, axis=2, keepdims=True)
    mean_removed = values - centre_mean
    variance = jnp.mean(mean_removed * mean_removed, axis=2, keepdims=True)
    reciprocal_deviation = lax.rsqrt(variance + 1e-06)
    standardized_input = mean_removed * reciprocal_deviation
    layer_normed = (standardized_input * gain).astype(jnp.bfloat16)
    pre_act = jnp.einsum("ufd,udr->ufr", layer_normed, w_down, preferred_element_type=jnp.float32)
    sigmoid_pre = jax.nn.sigmoid(pre_act)
    hidden = (pre_act * sigmoid_pre).astype(jnp.bfloat16)
    masked_up = jnp.where(live_mask, cotangent, jnp.zeros_like(cotangent))
    hidden_slots = hidden[None] * slot_select[:, :, None, None]
    grad_up = jnp.einsum(
        "ufd,sufr->sdr", masked_up, hidden_slots, preferred_element_type=jnp.float32
    )
    d_hidden = jnp.einsum("ufd,udr->ufr", masked_up, w_up, preferred_element_type=jnp.float32)
    d_pre = (d_hidden * sigmoid_pre * (1.0 + pre_act * (1.0 - sigmoid_pre))).astype(jnp.bfloat16)
    d_pre_slots = d_pre[None] * slot_select[:, :, None, None]
    grad_down = jnp.einsum(
        "ufd,sufr->sdr", layer_normed, d_pre_slots, preferred_element_type=jnp.float32
    )
    d_normed = jnp.einsum("ufr,udr->ufd", d_pre, w_down, preferred_element_type=jnp.float32)
    scaled_rows = d_normed * gain
    inner_gradient = (
        scaled_rows
        - jnp.mean(scaled_rows, axis=2, keepdims=True)
        - standardized_input * jnp.mean(scaled_rows * standardized_input, axis=2, keepdims=True)
    ) * reciprocal_deviation
    d_frames = (cotangent.astype(jnp.float32) + inner_gradient).astype(jnp.bfloat16)
    return (d_frames, grad_down, grad_up)


def on_device(frames, cotangent, gain, down_weight, up_weight, slot_lang, utt_slot, lengths):
    devices = lax.axis_size("dp")
    self_index = lax.axis_index("dp")
    per_device = frames.shape[0]
    slots = slot_lang.shape[1]
    lang_count, row_count, bottleneck = down_weight.shape
    owners = jnp.arange(utt_slot.shape[0], dtype=jnp.int32) // per_device
    utt_lang = slot_lang[owners, utt_slot]
    own_lengths = lax.dynamic_slice_in_dim(lengths, self_index * per_device, per_device)
    own_slot = lax.dynamic_slice_in_dim(utt_slot, self_index * per_device, per_device)
    live_mask = (jnp.arange(frames.shape[1], dtype=jnp.int32)[None, :] < own_lengths[:, None])[
        :, :, None
    ]
    lang_ids = jnp.arange(lang_count, dtype=jnp.int32)
    counts = jnp.sum(jnp.where(utt_lang[None, :] == lang_ids[:, None], lengths[None, :], 0), axis=1)
    scaling = lax.rsqrt(jnp.maximum(counts, 1).astype(jnp.float32))
    member_langs = slot_lang.T.reshape(-1)
    send_down = jnp.take(down_weight, member_langs, axis=0).reshape(
        slots, devices, row_count, bottleneck
    )
    send_up = jnp.take(up_weight, member_langs, axis=0).reshape(
        slots, devices, row_count, bottleneck
    )
    got_down = lax.all_to_all(send_down, "dp", split_axis=1, concat_axis=1, tiled=True)
    got_up = lax.all_to_all(send_up, "dp", split_axis=1, concat_axis=1, tiled=True)
    got_down = got_down.reshape(slots, devices * row_count, bottleneck)
    got_up = got_up.reshape(slots, devices * row_count, bottleneck)
    w_down = jnp.take(got_down, own_slot, axis=0)
    w_up = jnp.take(got_up, own_slot, axis=0)
    slot_select = (jnp.arange(slots, dtype=jnp.int32)[:, None] == own_slot[None, :]).astype(
        jnp.bfloat16
    )
    d_frames, grad_down, grad_up = local_pass(
        frames, cotangent, gain, w_down, w_up, live_mask, slot_select
    )
    own_scale = jnp.take(scaling, lax.dynamic_index_in_dim(slot_lang, self_index, 0, False))
    own_scale = own_scale[:, None, None]

    def exchange_back(grad):
        scaled = (grad * own_scale).astype(jnp.bfloat16)
        scaled = scaled.reshape(slots, devices, row_count, bottleneck)
        back = lax.all_to_all(scaled, "dp", split_axis=1, concat_axis=1, tiled=True)
        return back.reshape(slots * devices, row_count, bottleneck)

    back_down = exchange_back(grad_down)
    back_up = exchange_back(grad_up)
    lang_table = (lang_ids[:, None] == member_langs[None, :]).astype(jnp.bfloat16)
    down_grads = jnp.einsum(
        "lm,mkr->lkr", lang_table, back_down, preferred_element_type=jnp.float32
    ).astype(jnp.bfloat16)
    up_grads = jnp.einsum(
        "lm,mkr->lkr", lang_table, back_up, preferred_element_type=jnp.float32
    ).astype(jnp.bfloat16)
    return (d_frames, down_grads, up_grads)


def solution(mesh):
    placed = (
        P(("groups", "dp"), None, None),
        P(("groups", "dp"), None, None),
        P(),
        P("groups", "dp", None),
        P("groups", "dp", None),
        P("groups", None),
        P("groups"),
        P("groups"),
    )
    return jax.shard_map(
        on_device,
        mesh=mesh,
        in_specs=placed,
        out_specs=(
            P(("groups", "dp"), None, None),
            P("groups", "dp", None),
            P("groups", "dp", None),
        ),
        check_vma=False,
    )
```

profile of v0, /device:TPU:13, one launch (start us, length us, event | category | flops | bytes accessed | tf_op | source)
XLA Modules:
  0.0 215.7 jit_solution(16785040773158458793)
XLA Ops:
  0.6 0.8 reshape.205
  1.4 3.9 %gather_fusion.4 = bf16[32,96,256]{2,1,0:T(8,128)(2,1)S(1)} fusion(bf16[160,96,256]{2,1,0:T(8,128)(2,1)} %param.15, s32[1024]{0:T(1024)S(1)} %pad_clamp_fusion.2), kind=kCustom, calls=%fused_computation.2.clone | custom fusion | bytes 3145856 | tf_op jit(solution)/shard_map/jit(_take)/gather | solution.py:57
  5.3 3.9 %gather_fusion.2 = bf16[32,96,256]{2,1,0:T(8,128)(2,1)S(1)} fusion(bf16[160,96,256]{2,1,0:T(8,128)(2,1)} %param.16, s32[1024]{0:T(1024)S(1)} %pad_clamp_fusion.2), kind=kCustom, calls=%fused_computation.clone | custom fusion | bytes 3145856 | tf_op jit(solution)/shard_map/jit(_take)/gather | solution.py:60
  9.2 1.5 broadcast_select_fusion.4
  10.7 1.3 copy.51
  12.0 6.6 %all-to-all-start.1 = ((bf16[2,16,96,256]{3,2,0,1:T(8,128)(2,1)}), bf16[2,16,96,256]{3,2,0,1:T(8,128)(2,1)}, u32[]{:S(2)}, u32[]{:S(2)}) async-start(bf16[2,16,96,256]{3,2,0,1:T(8,128)(2,1)} %copy.51), calls=%async_computation.1 | async-start | bytes 3145728 | tf_op jit(solution)/shard_map/all_to_all | solution.py:63
  18.5 0.0 copy-start
  18.5 0.0 copy-start.6
  18.5 0.0 copy-start.1
  18.6 2.8 %copy.49 = bf16[2,16,96,256]{3,2,0,1:T(8,128)(2,1)} copy(bf16[2,16,96,256]{3,2,1,0:T(8,128)(2,1)} %bitcast.69) | data formatting | bytes 3145728 | tf_op jit(solution)/shard_map/reshape | solution.py:60
  21.4 33.4 %all-to-all-done.1 = bf16[2,16,96,256]{3,2,0,1:T(8,128)(2,1)} async-done(((bf16[2,16,96,256]{3,2,0,1:T(8,128)(2,1)}), bf16[2,16,96,256]{3,2,0,1:T(8,128)(2,1)}, u32[]{:S(2)}, u32[]{:S(2)}) %all-to-all-start.1) | async-done | bytes 1572896 | tf_op jit(solution)/shard_map/all_to_all | solution.py:63
  54.8 4.9 %all-to-all-start = ((bf16[2,16,96,256]{3,2,0,1:T(8,128)(2,1)}), bf16[2,16,96,256]{3,2,0,1:T(8,128)(2,1)}, u32[]{:S(2)}, u32[]{:S(2)}) async-start(bf16[2,16,96,256]{3,2,0,1:T(8,128)(2,1)} %copy.49), calls=%async_computation | async-start | bytes 3145728 | tf_op jit(solution)/shard_map/all_to_all | solution.py:64
  59.7 0.2 dynamic-slice_reduce_fusion
  59.9 0.9 gather_fusion
  60.8 0.1 dynamic_slice.10
  60.9 0.1 select_reduce_fusion
  61.0 0.6 gather_fusion.1
  61.7 0.1 compare_and_fusion
  61.8 0.1 iota_compare_fusion.2
  61.9 0.5 convert_reduce_fusion
  62.3 1.0 fusion.11
  63.3 2.7 %copy.52 = bf16[2,16,96,256]{3,2,1,0:T(8,128)(2,1)} copy(bf16[2,16,96,256]{3,2,0,1:T(8,128)(2,1)} %all-to-all-done.1) | data formatting | bytes 3145728 | tf_op jit(solution)/shard_map/all_to_all | solution.py:63
  66.0 3.8 %gather_fusion.5 = bf16[4,1536,256]{2,1,0:T(8,128)(2,1)} fusion(bf16[2,1536,256]{2,1,0:T(8,128)(2,1)} %bitcast.64, s32[1024]{0:T(1024)S(1)} %pad_clamp_fusion.1), kind=kCustom, calls=%fused_computation.3.clone | custom fusion | bytes 6291472 | tf_op jit(solution)/shard_map/jit(_take)/gather | solution.py:67
  69.8 26.2 %all-to-all-done = bf16[2,16,96,256]{3,2,0,1:T(8,128)(2,1)} async-done(((bf16[2,16,96,256]{3,2,0,1:T(8,128)(2,1)}), bf16[2,16,96,256]{3,2,0,1:T(8,128)(2,1)}, u32[]{:S(2)}, u32[]{:S(2)}) %all-to-all-start) | async-done | bytes 1572896 | tf_op jit(solution)/shard_map/all_to_all | solution.py:64
  96.0 2.7 %copy.50 = bf16[2,16,96,256]{3,2,1,0:T(8,128)(2,1)} copy(bf16[2,16,96,256]{3,2,0,1:T(8,128)(2,1)} %all-to-all-done) | data formatting | bytes 3145728 | tf_op jit(solution)/shard_map/all_to_all | solution.py:64
  98.7 3.8 %gather_fusion.3 = bf16[4,1536,256]{2,1,0:T(8,128)(2,1)} fusion(bf16[2,1536,256]{2,1,0:T(8,128)(2,1)} %bitcast.63, s32[1024]{0:T(1024)S(1)} %pad_clamp_fusion.1), kind=kCustom, calls=%fused_computation.1.clone | custom fusion | bytes 6291472 | tf_op jit(solution)/shard_map/jit(_take)/gather | solution.py:68
  102.5 4.4 %multiply_convert_fusion = (bf16[4,256,256]{2,1,0:T(8,128)(2,1)}, f32[4,256,256]{2,1,0:T(8,128)S(1)}) fusion(bf16[4,1536,256]{2,1,0:T(8,128)(2,1)} %gather_fusion.5, pred[4]{0:T(512)(128)(4,1)S(1)} %get-tuple-element.22, bf16[4,256,1536]{2,1,0:T(8,128)(2,1)S(1)} %copy-done.1, f32[1536]{0:T(1024)S(1)} %copy-done.5, f32[4,256]{1,0:T(4,128)S(1)} %add_rsqrt_fusion, ...), kind=kOutput, calls=%fused_computation.49 | convolution fusion | flops 816054272 | bytes 7878660 | tf_op jit(solution)/shard_map/ufd,udr->ufr/dot_general | solution.py:15
  106.9 2.2 %fusion.43 = bf16[4,256,256]{2,1,0:T(8,128)(2,1)} fusion(bf16[4,1536,256]{2,1,0:T(8,128)(2,1)S(1)} %copy-done.2, pred[4]{0:T(512)(128)(4,1)S(1)} %get-tuple-element.22, bf16[4,256,1536]{2,1,0:T(8,128)(2,1)S(1)} %copy-done.3, pred[4,256]{1,0:T(4,128)(4,1)S(1)} %iota_compare_fusion.2, f32[4,256,256]{2,1,0:T(8,128)S(1)} %get-tuple-element.28), kind=kOutput, calls=%fused_computation.46 | convolution fusion | flops 810811392 | bytes 7865348 | tf_op jit(solution)/shard_map/ufd,udr->ufr/dot_general | solution.py:23
  109.1 2.0 copy.53
  111.1 4.2 %fusion.28 = bf16[2,1536,256]{1,2,0:T(8,128)(2,1)} fusion(bf16[4,256,1536]{2,1,0:T(8,128)(2,1)S(1)} %copy-done.1, f32[1536]{0:T(1024)S(1)} %copy-done.5, f32[4,256]{1,0:T(4,128)S(1)} %add_rsqrt_fusion, f32[4,256]{1,0:T(4,128)S(1)} %broadcast_multiply_fusion.2, f32[2]{0:T(128)S(1)} %and_select_fusion.1, bf16[2,4]{1,0:T(2,128)(2,1)S(1)} %compare_convert_fusion, ...), kind=kOutput, calls=%fused_computation.37 | convolution fusion | flops 1620574208 | bytes 5257240 | tf_op jit(solution)/shard_map/ufd,sufr->sdr/dot_general | solution.py:26
  115.4 2.6 %copy.54 = bf16[2,1536,256]{2,1,0:T(8,128)(2,1)} copy(bf16[2,1536,256]{1,2,0:T(8,128)(2,1)} %fusion.28) | data formatting | bytes 3145728 | tf_op jit(solution)/shard_map/convert_element_type | solution.py:79
  117.9 2.7 %copy.55 = bf16[2,16,96,256]{3,2,0,1:T(8,128)(2,1)} copy(bf16[2,16,96,256]{3,2,1,0:T(8,128)(2,1)} %bitcast.66) | data formatting | bytes 3145728 | tf_op jit(solution)/shard_map/reshape | solution.py:80
  120.6 4.9 %all-to-all-start.2 = ((bf16[2,16,96,256]{3,2,0,1:T(8,128)(2,1)}), bf16[2,16,96,256]{3,2,0,1:T(8,128)(2,1)}, u32[]{:S(2)}, u32[]{:S(2)}) async-start(bf16[2,16,96,256]{3,2,0,1:T(8,128)(2,1)} %copy.55), calls=%async_computation.2 | async-start | bytes 3145728 | tf_op jit(solution)/shard_map/all_to_all | solution.py:81
  125.5 2.0 copy.57
  127.6 5.1 %fusion.25 = bf16[2,1536,256]{1,2,0:T(8,128)(2,1)} fusion(bf16[4,256,1536]{2,1,0:T(8,128)(2,1)} %param.13, pred[4,256]{1,0:T(4,128)(4,1)S(1)} %iota_compare_fusion.2, f32[2]{0:T(128)S(1)} %and_select_fusion.1, bf16[4,256,256]{1,2,0:T(8,128)(2,1)} %copy.57, bf16[2,4]{1,0:T(2,128)(2,1)S(1)} %compare_convert_fusion), kind=kOutput, calls=%fused_computation.36 | convolution fusion | flops 1614282752 | bytes 5243928 | tf_op jit(solution)/shard_map/ufd,sufr->sdr/dot_general | solution.py:20
  132.6 2.6 %copy.58 = bf16[2,1536,256]{2,1,0:T(8,128)(2,1)} copy(bf16[2,1536,256]{1,2,0:T(8,128)(2,1)} %fusion.25) | data formatting | bytes 3145728 | tf_op jit(solution)/shard_map/convert_element_type | solution.py:79
  135.2 2.7 %copy.59 = bf16[2,16,96,256]{3,2,0,1:T(8,128)(2,1)} copy(bf16[2,16,96,256]{3,2,1,0:T(8,128)(2,1)} %bitcast.67) | data formatting | bytes 3145728 | tf_op jit(solution)/shard_map/reshape | solution.py:80
  137.9 23.9 %all-to-all-done.2 = bf16[2,16,96,256]{3,2,0,1:T(8,128)(2,1)} async-done(((bf16[2,16,96,256]{3,2,0,1:T(8,128)(2,1)}), bf16[2,16,96,256]{3,2,0,1:T(8,128)(2,1)}, u32[]{:S(2)}, u32[]{:S(2)}) %all-to-all-start.2) | async-done | bytes 1572896 | tf_op jit(solution)/shard_map/all_to_all | solution.py:81
  161.8 4.9 %all-to-all-start.3 = ((bf16[2,16,96,256]{3,2,0,1:T(8,128)(2,1)}), bf16[2,16,96,256]{3,2,0,1:T(8,128)(2,1)}, u32[]{:S(2)}, u32[]{:S(2)}) async-start(bf16[2,16,96,256]{3,2,0,1:T(8,128)(2,1)} %copy.59), calls=%async_computation.3 | async-start | bytes 3145728 | tf_op jit(solution)/shard_map/all_to_all | solution.py:81
  166.7 4.6 %multiply_reduce_fusion = (f32[4,256]{1,0:T(4,128)S(1)}, f32[4,256]{1,0:T(4,128)S(1)}, f32[4,256,1536]{2,1,0:T(8,128)S(1)}) fusion(f32[1536]{0:T(1024)S(1)} %copy-done.5, f32[4,256]{1,0:T(4,128)S(1)} %add_rsqrt_fusion, f32[4,256]{1,0:T(4,128)S(1)} %broadcast_multiply_fusion.2, bf16[4,256,1536]{2,1,0:T(8,128)(2,1)S(1)} %copy-done.1, ...), kind=kOutput, calls=%fused_computation.22 | convolution fusion | flops 817887232 | bytes 13129732 | tf_op jit(solution)/shard_map/ufr,udr->ufd/dot_general | solution.py:29
  171.4 4.0 %fusion.10 = bf16[4,256,1536]{2,1,0:T(8,128)(2,1)} fusion(bf16[4,256,1536]{2,1,0:T(8,128)(2,1)S(1)} %copy-done.1, bf16[4,256,1536]{2,1,0:T(8,128)(2,1)S(1)} %copy-done.4, f32[4,256,1536]{2,1,0:T(8,128)S(1)} %get-tuple-element.26, f32[4,256]{1,0:T(4,128)S(1)} %get-tuple-element.29, f32[4,256]{1,0:T(4,128)S(1)} %get-tuple-element.30, f32[1536]{0:T(1024)S(1)} %copy-done.5, ...), kind=kLoop, calls=%fused_computation.20 | loop fusion | flops 17301504 | bytes 15751168 | tf_op jit(solution)/shard_map/convert_element_type | solution.py:36
  175.3 2.3 %copy.56 = bf16[2,16,96,256]{3,1,0,2:T(8,128)(2,1)S(1)} copy(bf16[2,16,96,256]{3,2,0,1:T(8,128)(2,1)} %all-to-all-done.2) | data formatting | bytes 3145728 | tf_op jit(solution)/shard_map/all_to_all | solution.py:81
  177.6 2.3 %convolution_convert_fusion.1 = bf16[160,96,256]{2,0,1:T(8,128)(2,1)S(1)} fusion(bf16[32,96,256]{2,0,1:T(8,128)(2,1)S(1)} %bitcast.68, s32[32]{0:T(128)S(1)} %reshape.205), kind=kOutput, calls=%fused_computation.14 | convolution fusion | flops 255595520 | bytes 9437312 | tf_op jit(solution)/shard_map/lm,mkr->lkr/dot_general | solution.py:87
  179.9 7.8 %copy.61 = bf16[160,96,256]{2,1,0:T(8,128)(2,1)} copy(bf16[160,96,256]{2,0,1:T(8,128)(2,1)S(1)} %convolution_convert_fusion.1) | data formatting | bytes 15728640
  187.7 15.3 %all-to-all-done.3 = bf16[2,16,96,256]{3,2,0,1:T(8,128)(2,1)} async-done(((bf16[2,16,96,256]{3,2,0,1:T(8,128)(2,1)}), bf16[2,16,96,256]{3,2,0,1:T(8,128)(2,1)}, u32[]{:S(2)}, u32[]{:S(2)}) %all-to-all-start.3) | async-done | bytes 1572896 | tf_op jit(solution)/shard_map/all_to_all | solution.py:81
  203.0 2.3 %copy.60 = bf16[2,16,96,256]{3,1,0,2:T(8,128)(2,1)S(1)} copy(bf16[2,16,96,256]{3,2,0,1:T(8,128)(2,1)} %all-to-all-done.3) | data formatting | bytes 3145728 | tf_op jit(solution)/shard_map/all_to_all | solution.py:81
  205.3 2.3 %convolution_convert_fusion = bf16[160,96,256]{2,0,1:T(8,128)(2,1)S(1)} fusion(bf16[32,96,256]{2,0,1:T(8,128)(2,1)S(1)} %bitcast.65, s32[32]{0:T(128)S(1)} %reshape.205), kind=kOutput, calls=%fused_computation.13 | convolution fusion | flops 255595520 | bytes 9437312 | tf_op jit(solution)/shard_map/lm,mkr->lkr/dot_general | solution.py:90
  207.6 8.1 %copy.62 = bf16[160,96,256]{2,1,0:T(8,128)(2,1)} copy(bf16[160,96,256]{2,0,1:T(8,128)(2,1)S(1)} %convolution_convert_fusion) | data formatting | bytes 15728640
  (27 shorter events, 0.1 us)
Async XLA Ops:
  12.0 42.8 %all-to-all-start.1 = ((bf16[2,16,96,256]{3,2,0,1:T(8,128)(2,1)}), bf16[2,16,96,256]{3,2,0,1:T(8,128)(2,1)}, u32[]{:S(2)}, u32[]{:S(2)}) async-start(bf16[2,16,96,256]{3,2,0,1:T(8,128)(2,1)} %copy.51), calls=%async_computation.1 | async-start | bytes 3145728 | tf_op jit(solution)/shard_map/all_to_all | solution.py:63
  18.5 41.2 %copy-start.7 = (s32[64]{0:T(128)S(1)}, s32[64]{0:T(128)}, u32[]{:S(2)}) copy-start(s32[64]{0:T(128)} %param.18) | copy-start | bytes 772
  18.5 41.2 %copy-start = (s32[16,2]{0,1:T(2,128)S(1)}, s32[16,2]{0,1:T(2,128)}, u32[]{:S(2)}) copy-start(s32[16,2]{0,1:T(2,128)} %param.17) | copy-start | bytes 388
  18.5 42.3 %copy-start.6 = (s32[64]{0:T(128)S(1)}, s32[64]{0:T(128)}, u32[]{:S(2)}) copy-start(s32[64]{0:T(128)} %param.19) | copy-start | bytes 772
  18.5 43.3 %copy-start.1 = (bf16[4,256,1536]{2,1,0:T(8,128)(2,1)S(1)}, bf16[4,256,1536]{2,1,0:T(8,128)(2,1)}, u32[]{:S(2)}) copy-start(bf16[4,256,1536]{2,1,0:T(8,128)(2,1)} %param.12) | copy-start | bytes 9437188
  54.8 41.2 %all-to-all-start = ((bf16[2,16,96,256]{3,2,0,1:T(8,128)(2,1)}), bf16[2,16,96,256]{3,2,0,1:T(8,128)(2,1)}, u32[]{:S(2)}, u32[]{:S(2)}) async-start(bf16[2,16,96,256]{3,2,0,1:T(8,128)(2,1)} %copy.49), calls=%async_computation | async-start | bytes 3145728 | tf_op jit(solution)/shard_map/all_to_all | solution.py:64
  98.7 3.8 %copy-start.5 = (f32[1536]{0:T(1024)S(1)}, f32[1536]{0:T(1024)}, u32[]{:S(2)}) copy-start(f32[1536]{0:T(1024)} %param.14) | copy-start | bytes 18436
  102.5 4.4 %copy-start.2 = (bf16[4,1536,256]{2,1,0:T(8,128)(2,1)S(1)}, bf16[4,1536,256]{2,1,0:T(8,128)(2,1)}, u32[]{:S(2)}) copy-start(bf16[4,1536,256]{2,1,0:T(8,128)(2,1)} %gather_fusion.3) | copy-start | bytes 9437188
  102.5 4.4 %copy-start.3 = (bf16[4,256,1536]{2,1,0:T(8,128)(2,1)S(1)}, bf16[4,256,1536]{2,1,0:T(8,128)(2,1)}, u32[]{:S(2)}) copy-start(bf16[4,256,1536]{2,1,0:T(8,128)(2,1)} %param.13) | copy-start | bytes 9437188
  120.6 41.2 %all-to-all-start.2 = ((bf16[2,16,96,256]{3,2,0,1:T(8,128)(2,1)}), bf16[2,16,96,256]{3,2,0,1:T(8,128)(2,1)}, u32[]{:S(2)}, u32[]{:S(2)}) async-start(bf16[2,16,96,256]{3,2,0,1:T(8,128)(2,1)} %copy.55), calls=%async_computation.2 | async-start | bytes 3145728 | tf_op jit(solution)/shard_map/all_to_all | solution.py:81
  161.8 41.2 %all-to-all-start.3 = ((bf16[2,16,96,256]{3,2,0,1:T(8,128)(2,1)}), bf16[2,16,96,256]{3,2,0,1:T(8,128)(2,1)}, u32[]{:S(2)}, u32[]{:S(2)}) async-start(bf16[2,16,96,256]{3,2,0,1:T(8,128)(2,1)} %copy.59), calls=%async_computation.3 | async-start | bytes 3145728 | tf_op jit(solution)/shard_map/all_to_all | solution.py:81
  166.7 4.6 %copy-start.4 = (bf16[4,256,1536]{2,1,0:T(8,128)(2,1)S(1)}, bf16[4,256,1536]{2,1,0:T(8,128)(2,1)}, u32[]{:S(2)}) copy-start(bf16[4,256,1536]{2,1,0:T(8,128)(2,1)} %param.13) | copy-start | bytes 9437188
where the time goes:
time: 217 us; the launch traced here: 216 us
  waiting for transfers between devices  98.8 us (46%)
  local copies, waits for them, and re-layouts  62.5 us (29%)
  matrix products  25.1 us (12%)
  starting transfers between devices  21.3 us (10%)
  other arithmetic  7.25 us (3%)
    all_to_all x2, waiting for transfers between devices, exchange_back(): back = lax.all_to_all(scaled, 'dp', split_axis=1, concat_axis=1, tiled=True)  39.2 us
    all_to_all x1, waiting for transfers between devices, on_device(): lax.all_to_all(send_down, 'dp', split_axis=1, concat_axis=1, tiled=True)  33.4 us
    all_to_all x1, waiting for transfers between devices, on_device(): lax.all_to_all(send_up, 'dp', split_axis=1, concat_axis=1, tiled=True)  26.2 us
    unnamed x18, local copies, waits for them, and re-layouts  15.9 us
    all_to_all x2, starting transfers between devices, exchange_back(): back = lax.all_to_all(scaled, 'dp', split_axis=1, concat_axis=1, tiled=True)  9.83 us
    all_to_all x1, starting transfers between devices, on_device(): lax.all_to_all(send_down, 'dp', split_axis=1, concat_axis=1, tiled=True)  6.55 us
    reshape x2, local copies, waits for them, and re-layouts, exchange_back(): scaled = scaled.reshape(slots, devices, row_count, bottleneck)  5.37 us
    convert_element_type x2, local copies, waits for them, and re-layouts, exchange_back(): scaled = (grad * own_scale).astype(jnp.bfloat16)  5.15 us
  transfers between devices with their start and end apart: 4, of which 4 were waited for; matrix products, arithmetic and copies ran while one was open for 21% of the time, Pallas kernels for 0%

commit v1 on v0

--- a/solution.py
+++ b/solution.py
@@ -2,6 +2,17 @@
 import jax.numpy as jnp
 from jax import lax
 from jax.sharding import PartitionSpec as P
+
+
+def in_blocks(x, dim, length):
+    before, after = (x.shape[:dim], x.shape[dim + 1 :])
+    return jnp.moveaxis(x.reshape(*before, length, -1, *after), dim, 0)
+
+
+def in_order(tiles, dim):
+    tiles = jnp.moveaxis(tiles, 0, dim)
+    shape = tiles.shape
+    return tiles.reshape(*shape[:dim], shape[dim] * shape[dim + 1], *shape[dim + 2 :])
 
 
 def local_pass(frames, cotangent, gain, w_down, w_up, live_mask, slot_select):
@@ -78,7 +89,14 @@
     def exchange_back(grad):
         scaled = (grad * own_scale).astype(jnp.bfloat16)
         scaled = scaled.reshape(slots, devices, row_count, bottleneck)
-        back = lax.all_to_all(scaled, "dp", split_axis=1, concat_axis=1, tiled=True)
+        count, index = (lax.axis_size("dp"), lax.axis_index("dp"))
+        pieces = in_blocks(scaled, 1, count)
+        outs = [pieces[index]]
+        for step in range(1, count):
+            sent = pieces[index ^ step]
+            outs.append(lax.ppermute(sent, "dp", [(i, i ^ step) for i in range(count)]))
+        pieces = jnp.stack(outs)[index ^ jnp.arange(count)]
+        back = in_order(pieces, 1)
         return back.reshape(slots * devices, row_count, bottleneck)
 
     back_down = exchange_back(grad_down)

time: 217 us -> 315 us (1.45)
  starting transfers between devices: 21.3 us -> 66.4 us
  local copies, waits for them, and re-layouts: 62.5 us -> 85.8 us
  waiting for transfers between devices: 98.8 us -> 122 us
    ppermute x0 -> x30, waiting for transfers between devices: none -> 60.3 us  [exchange_back(): outs.append(lax.ppermute(sent, 'dp', [(i, i ^ step) for i in range(count)]))]
    ppermute x0 -> x30, starting transfers between devices: none -> 54.9 us  [exchange_back(): outs.append(lax.ppermute(sent, 'dp', [(i, i ^ step) for i in range(count)]))]
    all_to_all x2 -> x0, waiting for transfers between devices: 39.2 us -> none  [exchange_back(): back = lax.all_to_all(scaled, 'dp', split_axis=1, concat_axis=1, tiled=True)]
    unnamed x18 -> x50, local copies, waits for them, and re-layouts: 15.9 us -> 36.3 us
    all_to_all x2 -> x0, starting transfers between devices: 9.83 us -> none  [exchange_back(): back = lax.all_to_all(scaled, 'dp', split_axis=1, concat_axis=1, tiled=True)]
    gather x0 -> x2, local copies, waits for them, and re-layouts: none -> 6.39 us  [exchange_back(): pieces = jnp.stack(outs)[index ^ jnp.arange(count)]]
    reshape x2 -> x0, local copies, waits for them, and re-layouts: 5.37 us -> none  [exchange_back(): scaled = scaled.reshape(slots, devices, row_count, bottleneck)]
    all_to_all x2 -> x0, local copies, waits for them, and re-layouts: 4.57 us -> none  [exchange_back(): back = lax.all_to_all(scaled, 'dp', split_axis=1, concat_axis=1, tiled=True)]
  transfers between devices with their start and end apart: 4 -> 32, of which waited for: 4 -> 23; matrix products, arithmetic and copies ran while one was open for 21% -> 13% of each run, Pallas kernels for 0% -> 0%
where the time goes in v1:
time: 315 us; the launch traced here: 311 us
  waiting for transfers between devices  122 us (39%)
  local copies, waits for them, and re-layouts  85.8 us (27%)
  starting transfers between devices  66.4 us (21%)
  matrix products  27.2 us (9%)
  other arithmetic  9.43 us (3%)
    ppermute x30, waiting for transfers between devices, exchange_back(): outs.append(lax.ppermute(sent, 'dp', [(i, i ^ step) for i in range(count)]))  60.3 us
    ppermute x30, starting transfers between devices, exchange_back(): outs.append(lax.ppermute(sent, 'dp', [(i, i ^ step) for i in range(count)]))  54.9 us
    unnamed x50, local copies, waits for them, and re-layouts  36.3 us
    all_to_all x1, waiting for transfers between devices, on_device(): lax.all_to_all(send_down, 'dp', split_axis=1, concat_axis=1, tiled=True)  35 us
    all_to_all x1, waiting for transfers between devices, on_device(): lax.all_to_all(send_up, 'dp', split_axis=1, concat_axis=1, tiled=True)  26.3 us
    dot_general x1, matrix products, local_pass(): jnp.einsum('ufr,udr->ufd', d_pre, w_down, preferred_element_type=jnp.floa...  6.84 us
    all_to_all x1, starting transfers between devices, on_device(): lax.all_to_all(send_down, 'dp', split_axis=1, concat_axis=1, tiled=True)  6.55 us
    gather x2, local copies, waits for them, and re-layouts, exchange_back(): pieces = jnp.stack(outs)[index ^ jnp.arange(count)]  6.39 us
  transfers between devices with their start and end apart: 32, of which 23 were waited for; matrix products, arithmetic and copies ran while one was open for 13% of the time, Pallas kernels for 0%

profile of v1, /device:TPU:13, one launch (start us, length us, event | category | flops | bytes accessed | tf_op | source)
XLA Modules:
  0.0 311.3 jit_solution(7232778948457226698)
XLA Ops:
  2.3 3.9 %gather_fusion.6 = bf16[32,96,256]{2,1,0:T(8,128)(2,1)S(1)} fusion(bf16[160,96,256]{2,1,0:T(8,128)(2,1)} %param.15, s32[1024]{0:T(1024)S(1)} %get-tuple-element.63), kind=kCustom, calls=%fused_computation.2.clone | custom fusion | bytes 3145856 | tf_op jit(solution)/shard_map/jit(_take)/gather | solution.py:68
  6.2 5.0 %gather_fusion.4 = bf16[32,96,256]{2,1,0:T(8,128)(2,1)} fusion(bf16[160,96,256]{2,1,0:T(8,128)(2,1)} %param.16, s32[1024]{0:T(1024)S(1)} %get-tuple-element.63), kind=kCustom, calls=%fused_computation.clone | custom fusion | bytes 3145856 | tf_op jit(solution)/shard_map/jit(_take)/gather | solution.py:71
  14.2 6.6 %all-to-all-start.1 = ((bf16[2,16,96,256]{3,2,0,1:T(8,128)(2,1)}), bf16[2,16,96,256]{3,2,0,1:T(8,128)(2,1)}, u32[]{:S(2)}, u32[]{:S(2)}) async-start(bf16[2,16,96,256]{3,2,0,1:T(8,128)(2,1)} %copy.65), calls=%async_computation.1 | async-start | bytes 3145728 | tf_op jit(solution)/shard_map/all_to_all | solution.py:74
  22.1 35.0 %all-to-all-done.1 = bf16[2,16,96,256]{3,2,0,1:T(8,128)(2,1)} async-done(((bf16[2,16,96,256]{3,2,0,1:T(8,128)(2,1)}), bf16[2,16,96,256]{3,2,0,1:T(8,128)(2,1)}, u32[]{:S(2)}, u32[]{:S(2)}) %all-to-all-start.1) | async-done | bytes 1572896 | tf_op jit(solution)/shard_map/all_to_all | solution.py:74
  57.1 4.9 %all-to-all-start = ((bf16[2,16,96,256]{3,2,0,1:T(8,128)(2,1)}), bf16[2,16,96,256]{3,2,0,1:T(8,128)(2,1)}, u32[]{:S(2)}, u32[]{:S(2)}) async-start(bf16[2,16,96,256]{3,2,0,1:T(8,128)(2,1)} %copy.63), calls=%async_computation | async-start | bytes 3145728 | tf_op jit(solution)/shard_map/all_to_all | solution.py:75
  65.5 2.7 copy.66
  68.2 3.8 %gather_fusion.7 = bf16[4,1536,256]{2,1,0:T(8,128)(2,1)} fusion(bf16[2,1536,256]{2,1,0:T(8,128)(2,1)} %bitcast.200, s32[1024]{0:T(1024)S(1)} %pad_clamp_fusion.2), kind=kCustom, calls=%fused_computation.3.clone | custom fusion | bytes 6291472 | tf_op jit(solution)/shard_map/jit(_take)/gather | solution.py:78
  72.0 26.3 %all-to-all-done = bf16[2,16,96,256]{3,2,0,1:T(8,128)(2,1)} async-done(((bf16[2,16,96,256]{3,2,0,1:T(8,128)(2,1)}), bf16[2,16,96,256]{3,2,0,1:T(8,128)(2,1)}, u32[]{:S(2)}, u32[]{:S(2)}) %all-to-all-start) | async-done | bytes 1572896 | tf_op jit(solution)/shard_map/all_to_all | solution.py:75
  98.3 2.7 copy.64
  100.9 3.8 %gather_fusion.5 = bf16[4,1536,256]{2,1,0:T(8,128)(2,1)} fusion(bf16[2,1536,256]{2,1,0:T(8,128)(2,1)} %bitcast.199, s32[1024]{0:T(1024)S(1)} %pad_clamp_fusion.2), kind=kCustom, calls=%fused_computation.1.clone | custom fusion | bytes 6291472 | tf_op jit(solution)/shard_map/jit(_take)/gather | solution.py:79
  104.8 4.4 %multiply_convert_fusion = (bf16[4,256,256]{2,1,0:T(8,128)(2,1)}, f32[4,256,256]{2,1,0:T(8,128)S(1)}) fusion(bf16[4,1536,256]{2,1,0:T(8,128)(2,1)} %gather_fusion.7, pred[4]{0:T(512)(128)(4,1)S(1)} %get-tuple-element.25, bf16[4,256,1536]{2,1,0:T(8,128)(2,1)S(1)} %copy-done.1, f32[1536]{0:T(1024)S(1)} %copy-done.6, f32[4,256]{1,0:T(4,128)S(1)} %add_rsqrt_fusion, ...), kind=kOutput, calls=%fused_computation.53 | convolution fusion | flops 816054272 | bytes 7878660 | tf_op jit(solution)/shard_map/ufd,udr->ufr/dot_general | solution.py:26
  109.2 2.2 fusion.45
  113.4 6.8 %multiply_reduce_fusion = (f32[4,256]{1,0:T(4,128)S(1)}, f32[4,256]{1,0:T(4,128)S(1)}, f32[4,256,1536]{2,1,0:T(8,128)}) fusion(f32[1536]{0:T(1024)S(1)} %copy-done.6, f32[4,256]{1,0:T(4,128)S(1)} %add_rsqrt_fusion, f32[4,256]{1,0:T(4,128)S(1)} %broadcast_multiply_fusion.2, bf16[4,256,1536]{2,1,0:T(8,128)(2,1)S(1)} %copy-done.1, ...), kind=kOutput, calls=%fused_computation.24 | convolution fusion | flops 817887232 | bytes 13129732 | tf_op jit(solution)/shard_map/ufr,udr->ufd/dot_general | solution.py:40
  122.3 5.1 %fusion.25 = bf16[2,1536,256]{1,2,0:T(8,128)(2,1)} fusion(bf16[4,256,1536]{2,1,0:T(8,128)(2,1)} %param.13, pred[4,256]{1,0:T(4,128)(4,1)S(1)} %iota_compare_fusion.2, f32[2]{0:T(128)S(1)} %and_select_fusion.1, bf16[4,256,256]{1,2,0:T(8,128)(2,1)} %copy.72, bf16[2,4]{1,0:T(2,128)(2,1)S(1)} %compare_convert_fusion), kind=kOutput, calls=%fused_computation.38 | convolution fusion | flops 1614282752 | bytes 5243928 | tf_op jit(solution)/shard_map/ufd,sufr->sdr/dot_general | solution.py:31
  127.4 2.6 copy.73
  129.9 4.1 %fusion.28 = bf16[2,1536,256]{1,2,0:T(8,128)(2,1)} fusion(bf16[4,256,1536]{2,1,0:T(8,128)(2,1)S(1)} %copy-done.1, f32[1536]{0:T(1024)S(1)} %copy-done.6, f32[4,256]{1,0:T(4,128)S(1)} %add_rsqrt_fusion, f32[4,256]{1,0:T(4,128)S(1)} %broadcast_multiply_fusion.2, f32[2]{0:T(128)S(1)} %and_select_fusion.1, bf16[2,4]{1,0:T(2,128)(2,1)S(1)} %compare_convert_fusion, ...), kind=kOutput, calls=%fused_computation.39 | convolution fusion | flops 1620574208 | bytes 5257240 | tf_op jit(solution)/shard_map/ufd,sufr->sdr/dot_general | solution.py:37
  134.1 2.6 copy.68
  144.9 5.9 %fusion.10 = bf16[4,256,1536]{2,1,0:T(8,128)(2,1)} fusion(bf16[4,256,1536]{2,1,0:T(8,128)(2,1)S(1)} %copy-done.1, bf16[4,256,1536]{2,1,0:T(8,128)(2,1)S(1)} %copy-done.5, f32[4,256,1536]{2,1,0:T(8,128)} %get-tuple-element.59, f32[4,256]{1,0:T(4,128)S(1)} %broadcast_multiply_fusion, f32[4,256]{1,0:T(4,128)S(1)} %broadcast_multiply_fusion.1, ...), kind=kLoop, calls=%fused_computation.22 | loop fusion | flops 17301504 | bytes 15751168 | tf_op jit(solution)/shard_map/convert_element_type | solution.py:47
  152.1 4.0 %collective-permute-done.1 = bf16[2,1,96,256]{3,2,0,1:T(8,128)(2,1)S(1)} collective-permute-done((bf16[2,1,96,256]{3,2,0,1:T(8,128)(2,1)S(1)}, bf16[2,1,96,256]{3,2,0,1:T(8,128)(2,1)S(1)}, u32[]{:S(2)}, u32[]{:S(2)}) %collective-permute-start.1) | collective-permute-done | bytes 98336 | tf_op jit(solution)/shard_map/ppermute | solution.py:97
  158.4 3.0 collective-permute-done.2
  161.4 2.5 collective-permute-start.3
  166.5 2.5 collective-permute-start.4
  169.6 2.4 collective-permute-done.4
  173.3 3.6 %collective-permute-done.5 = bf16[2,1,96,256]{3,2,0,1:T(8,128)(2,1)S(1)} collective-permute-done((bf16[2,1,96,256]{3,2,0,1:T(8,128)(2,1)S(1)}, bf16[2,1,96,256]{3,2,0,1:T(8,128)(2,1)S(1)}, u32[]{:S(2)}, u32[]{:S(2)}) %collective-permute-start.5) | collective-permute-done | bytes 98336 | tf_op jit(solution)/shard_map/ppermute | solution.py:97
  179.5 3.1 %collective-permute-done.6 = bf16[2,1,96,256]{3,2,0,1:T(8,128)(2,1)S(1)} collective-permute-done((bf16[2,1,96,256]{3,2,0,1:T(8,128)(2,1)S(1)}, bf16[2,1,96,256]{3,2,0,1:T(8,128)(2,1)S(1)}, u32[]{:S(2)}, u32[]{:S(2)}) %collective-permute-start.6) | collective-permute-done | bytes 98336 | tf_op jit(solution)/shard_map/ppermute | solution.py:97
  184.0 3.1 collective-permute-done.7
  187.1 5.4 %collective-permute-start.8 = (bf16[2,1,96,256]{3,2,0,1:T(8,128)(2,1)S(1)}, bf16[2,1,96,256]{3,2,0,1:T(8,128)(2,1)S(1)}, u32[]{:S(2)}, u32[]{:S(2)}) collective-permute-start(bf16[2,1,96,256]{3,2,0,1:T(8,128)(2,1)S(1)} %get-tuple-element.48), channel_id=1, source_target_pairs={{0,9},{1,8},{2,11},{3,10},{4,13},{5,12},{6,15},{7,14},{8,1},{9,0},... | collective-permute-start | bytes 294920 | tf_op jit(solution)/shard_map/ppermute | solution.py:97
  195.8 5.5 %collective-permute-done.9 = bf16[2,1,96,256]{3,2,0,1:T(8,128)(2,1)S(1)} collective-permute-done((bf16[2,1,96,256]{3,2,0,1:T(8,128)(2,1)S(1)}, bf16[2,1,96,256]{3,2,0,1:T(8,128)(2,1)S(1)}, u32[]{:S(2)}, u32[]{:S(2)}) %collective-permute-start.9) | collective-permute-done | bytes 98336 | tf_op jit(solution)/shard_map/ppermute | solution.py:97
  201.3 4.7 %collective-permute-start.10 = (bf16[2,1,96,256]{3,2,0,1:T(8,128)(2,1)S(1)}, bf16[2,1,96,256]{3,2,0,1:T(8,128)(2,1)S(1)}, u32[]{:S(2)}, u32[]{:S(2)}) collective-permute-start(bf16[2,1,96,256]{3,2,0,1:T(8,128)(2,1)S(1)} %get-tuple-element.46), channel_id=1, source_target_pairs={{0,11},{1,10},{2,9},{3,8},{4,15},{5,14},{6,13},{7,12},{8,3},{9,2},... | collective-permute-start | bytes 294920 | tf_op jit(solution)/shard_map/ppermute | solution.py:97
  218.4 3.4 %collective-permute-done.16 = bf16[2,1,96,256]{3,2,0,1:T(8,128)(2,1)S(1)} collective-permute-done((bf16[2,1,96,256]{3,2,0,1:T(8,128)(2,1)S(1)}, bf16[2,1,96,256]{3,2,0,1:T(8,128)(2,1)S(1)}, u32[]{:S(2)}, u32[]{:S(2)}) %collective-permute-start.16) | collective-permute-done | bytes 98336 | tf_op jit(solution)/shard_map/ppermute | solution.py:97
  224.1 3.1 collective-permute-done.17
  227.1 5.7 %collective-permute-start.18 = (bf16[2,1,96,256]{3,2,0,1:T(8,128)(2,1)S(1)}, bf16[2,1,96,256]{3,2,0,1:T(8,128)(2,1)S(1)}, u32[]{:S(2)}, u32[]{:S(2)}) collective-permute-start(bf16[2,1,96,256]{3,2,0,1:T(8,128)(2,1)S(1)} %get-tuple-element.38), channel_id=1, source_target_pairs={{0,4},{1,5},{2,6},{3,7},{4,0},{5,1},{6,2},{7,3},{8,12},{9,13},{10,... | collective-permute-start | bytes 294920 | tf_op jit(solution)/shard_map/ppermute | solution.py:97
  235.2 3.0 collective-permute-start.19
  238.9 2.2 collective-permute-done.19
  241.7 4.4 %collective-permute-done.20 = bf16[2,1,96,256]{3,2,0,1:T(8,128)(2,1)S(1)} collective-permute-done((bf16[2,1,96,256]{3,2,0,1:T(8,128)(2,1)S(1)}, bf16[2,1,96,256]{3,2,0,1:T(8,128)(2,1)S(1)}, u32[]{:S(2)}, u32[]{:S(2)}) %collective-permute-start.20) | collective-permute-done | bytes 98336 | tf_op jit(solution)/shard_map/ppermute | solution.py:97
  248.9 3.2 %collective-permute-done.21 = bf16[2,1,96,256]{3,2,0,1:T(8,128)(2,1)S(1)} collective-permute-done((bf16[2,1,96,256]{3,2,0,1:T(8,128)(2,1)S(1)}, bf16[2,1,96,256]{3,2,0,1:T(8,128)(2,1)S(1)}, u32[]{:S(2)}, u32[]{:S(2)}) %collective-permute-start.21) | collective-permute-done | bytes 98336 | tf_op jit(solution)/shard_map/ppermute | solution.py:97
  252.8 3.8 %collective-permute-done.22 = bf16[2,1,96,256]{3,2,0,1:T(8,128)(2,1)S(1)} collective-permute-done((bf16[2,1,96,256]{3,2,0,1:T(8,128)(2,1)S(1)}, bf16[2,1,96,256]{3,2,0,1:T(8,128)(2,1)S(1)}, u32[]{:S(2)}, u32[]{:S(2)}) %collective-permute-start.22) | collective-permute-done | bytes 98336 | tf_op jit(solution)/shard_map/ppermute | solution.py:97
  256.6 4.1 %collective-permute-start.23 = (bf16[2,1,96,256]{3,2,0,1:T(8,128)(2,1)S(1)}, bf16[2,1,96,256]{3,2,0,1:T(8,128)(2,1)S(1)}, u32[]{:S(2)}, u32[]{:S(2)}) collective-permute-start(bf16[2,1,96,256]{3,2,0,1:T(8,128)(2,1)S(1)} %get-tuple-element.33), channel_id=1, source_target_pairs={{0,9},{1,8},{2,11},{3,10},{4,13},{5,12},{6,15},{7,14},{8,1},{9,0},... | collective-permute-start | bytes 294920 | tf_op jit(solution)/shard_map/ppermute | solution.py:97
  261.3 2.4 collective-permute-done.23
  263.7 4.2 %collective-permute-start.24 = (bf16[2,1,96,256]{3,2,0,1:T(8,128)(2,1)S(1)}, bf16[2,1,96,256]{3,2,0,1:T(8,128)(2,1)S(1)}, u32[]{:S(2)}, u32[]{:S(2)}) collective-permute-start(bf16[2,1,96,256]{3,2,0,1:T(8,128)(2,1)S(1)} %get-tuple-element.32), channel_id=1, source_target_pairs={{0,10},{1,11},{2,8},{3,9},{4,14},{5,15},{6,12},{7,13},{8,2},{9,3},... | collective-permute-start | bytes 294920 | tf_op jit(solution)/shard_map/ppermute | solution.py:97
  270.7 4.1 %collective-permute-start.25 = (bf16[2,1,96,256]{3,2,0,1:T(8,128)(2,1)S(1)}, bf16[2,1,96,256]{3,2,0,1:T(8,128)(2,1)S(1)}, u32[]{:S(2)}, u32[]{:S(2)}) collective-permute-start(bf16[2,1,96,256]{3,2,0,1:T(8,128)(2,1)S(1)} %get-tuple-element.31), channel_id=1, source_target_pairs={{0,11},{1,10},{2,9},{3,8},{4,15},{5,14},{6,13},{7,12},{8,3},{9,2},... | collective-permute-start | bytes 294920 | tf_op jit(solution)/shard_map/ppermute | solution.py:97
  275.5 2.6 collective-permute-done.25
  280.7 3.2 %gather_fusion.2 = bf16[16,2,96,256]{3,2,1,0:T(8,128)(2,1)} fusion(bf16[16,2,96,256]{3,2,1,0:T(8,128)(2,1)} %bitcast.46, s32[1024]{0:T(1024)S(1)} %pad_clamp_fusion), kind=kCustom, calls=%fused_computation.6 | custom fusion | bytes 3145792 | tf_op jit(solution)/shard_map/gather | solution.py:98
  286.1 3.2 %gather_fusion.3 = bf16[16,2,96,256]{3,2,1,0:T(8,128)(2,1)} fusion(bf16[16,2,96,256]{3,2,1,0:T(8,128)(2,1)} %bitcast.88, s32[1024]{0:T(1024)S(1)} %pad_clamp_fusion), kind=kCustom, calls=%fused_computation.7 | custom fusion | bytes 3145792 | tf_op jit(solution)/shard_map/gather | solution.py:98
  290.8 2.3 convolution_convert_fusion
  293.1 7.8 %copy.78 = bf16[160,96,256]{2,1,0:T(8,128)(2,1)} copy(bf16[160,96,256]{2,0,1:T(8,128)(2,1)S(1)} %convolution_convert_fusion) | data formatting | bytes 15728640
  301.0 2.3 convolution_convert_fusion.1
  303.3 8.1 %copy.77 = bf16[160,96,256]{2,1,0:T(8,128)(2,1)} copy(bf16[160,96,256]{2,0,1:T(8,128)(2,1)S(1)} %convolution_convert_fusion.1) | data formatting | bytes 15728640
  (121 shorter events, 69.3 us)
Async XLA Ops:
  14.2 42.8 %all-to-all-start.1 = ((bf16[2,16,96,256]{3,2,0,1:T(8,128)(2,1)}), bf16[2,16,96,256]{3,2,0,1:T(8,128)(2,1)}, u32[]{:S(2)}, u32[]{:S(2)}) async-start(bf16[2,16,96,256]{3,2,0,1:T(8,128)(2,1)} %copy.65), calls=%async_computation.1 | async-start | bytes 3145728 | tf_op jit(solution)/shard_map/all_to_all | solution.py:74
  20.8 41.2 %copy-start.8 = (s32[64]{0:T(128)S(1)}, s32[64]{0:T(128)}, u32[]{:S(2)}) copy-start(s32[64]{0:T(128)} %param.18) | copy-start | bytes 772
  22.1 40.0 %copy-start = (s32[16,2]{0,1:T(2,128)S(1)}, s32[16,2]{0,1:T(2,128)}, u32[]{:S(2)}) copy-start(s32[16,2]{0,1:T(2,128)} %param.17) | copy-start | bytes 388
  22.1 40.9 %copy-start.7 = (s32[64]{0:T(128)S(1)}, s32[64]{0:T(128)}, u32[]{:S(2)}) copy-start(s32[64]{0:T(128)} %param.19) | copy-start | bytes 772
  22.1 42.0 %copy-start.1 = (bf16[4,256,1536]{2,1,0:T(8,128)(2,1)S(1)}, bf16[4,256,1536]{2,1,0:T(8,128)(2,1)}, u32[]{:S(2)}) copy-start(bf16[4,256,1536]{2,1,0:T(8,128)(2,1)} %param.12) | copy-start | bytes 9437188
  57.1 41.2 %all-to-all-start = ((bf16[2,16,96,256]{3,2,0,1:T(8,128)(2,1)}), bf16[2,16,96,256]{3,2,0,1:T(8,128)(2,1)}, u32[]{:S(2)}, u32[]{:S(2)}) async-start(bf16[2,16,96,256]{3,2,0,1:T(8,128)(2,1)} %copy.63), calls=%async_computation | async-start | bytes 3145728 | tf_op jit(solution)/shard_map/all_to_all | solution.py:75
  100.9 3.8 %copy-start.6 = (f32[1536]{0:T(1024)S(1)}, f32[1536]{0:T(1024)}, u32[]{:S(2)}) copy-start(f32[1536]{0:T(1024)} %param.14) | copy-start | bytes 18436
  104.8 4.4 %copy-start.3 = (bf16[4,1536,256]{2,1,0:T(8,128)(2,1)S(1)}, bf16[4,1536,256]{2,1,0:T(8,128)(2,1)}, u32[]{:S(2)}) copy-start(bf16[4,1536,256]{2,1,0:T(8,128)(2,1)} %gather_fusion.5) | copy-start | bytes 9437188
  104.8 4.4 %copy-start.4 = (bf16[4,256,1536]{2,1,0:T(8,128)(2,1)S(1)}, bf16[4,256,1536]{2,1,0:T(8,128)(2,1)}, u32[]{:S(2)}) copy-start(bf16[4,256,1536]{2,1,0:T(8,128)(2,1)} %param.13) | copy-start | bytes 9437188
  136.7 8.0 %copy-start.2 = (bf16[2,1536,256]{2,1,0:T(8,128)(2,1)S(1)}, bf16[2,1536,256]{2,1,0:T(8,128)(2,1)}, u32[]{:S(2)}) copy-start(bf16[2,1536,256]{2,1,0:T(8,128)(2,1)} %copy.73) | copy-start | bytes 4718596
  138.3 6.6 %copy-start.5 = (bf16[4,256,1536]{2,1,0:T(8,128)(2,1)S(1)}, bf16[4,256,1536]{2,1,0:T(8,128)(2,1)}, u32[]{:S(2)}) copy-start(bf16[4,256,1536]{2,1,0:T(8,128)(2,1)} %param.13) | copy-start | bytes 9437188
  140.0 75.8 %collective-permute-start.14 = (bf16[2,1,96,256]{3,2,0,1:T(8,128)(2,1)S(1)}, bf16[2,1,96,256]{3,2,0,1:T(8,128)(2,1)S(1)}, u32[]{:S(2)}, u32[]{:S(2)}) collective-permute-start(bf16[2,1,96,256]{3,2,0,1:T(8,128)(2,1)S(1)} %get-tuple-element.42), channel_id=1, source_target_pairs={{0,15},{1,14},{2,13},{3,12},{4,11},{5,10},{6,9},{7,8},{8,7},{9,6},... | collective-permute-start | bytes 294920 | tf_op jit(solution)/shard_map/ppermute | solution.py:97
  141.7 73.0 %collective-permute-start.13 = (bf16[2,1,96,256]{3,2,0,1:T(8,128)(2,1)S(1)}, bf16[2,1,96,256]{3,2,0,1:T(8,128)(2,1)S(1)}, u32[]{:S(2)}, u32[]{:S(2)}) collective-permute-start(bf16[2,1,96,256]{3,2,0,1:T(8,128)(2,1)S(1)} %get-tuple-element.43), channel_id=1, source_target_pairs={{0,14},{1,15},{2,12},{3,13},{4,10},{5,11},{6,8},{7,9},{8,6},{9,7},... | collective-permute-start | bytes 294920 | tf_op jit(solution)/shard_map/ppermute | solution.py:97
  142.5 69.7 %collective-permute-start.12 = (bf16[2,1,96,256]{3,2,0,1:T(8,128)(2,1)S(1)}, bf16[2,1,96,256]{3,2,0,1:T(8,128)(2,1)S(1)}, u32[]{:S(2)}, u32[]{:S(2)}) collective-permute-start(bf16[2,1,96,256]{3,2,0,1:T(8,128)(2,1)S(1)} %get-tuple-element.44), channel_id=1, source_target_pairs={{0,13},{1,12},{2,15},{3,14},{4,9},{5,8},{6,11},{7,10},{8,5},{9,4},... | collective-permute-start | bytes 294920 | tf_op jit(solution)/shard_map/ppermute | solution.py:97
  142.5 69.0 %collective-permute-start.11 = (bf16[2,1,96,256]{3,2,0,1:T(8,128)(2,1)S(1)}, bf16[2,1,96,256]{3,2,0,1:T(8,128)(2,1)S(1)}, u32[]{:S(2)}, u32[]{:S(2)}) collective-permute-start(bf16[2,1,96,256]{3,2,0,1:T(8,128)(2,1)S(1)} %get-tuple-element.45), channel_id=1, source_target_pairs={{0,12},{1,13},{2,14},{3,15},{4,8},{5,9},{6,10},{7,11},{8,4},{9,5},... | collective-permute-start | bytes 294920 | tf_op jit(solution)/shard_map/ppermute | solution.py:97
  144.5 6.9 %collective-permute-start = (bf16[2,1,96,256]{3,2,0,1:T(8,128)(2,1)S(1)}, bf16[2,1,96,256]{3,2,0,1:T(8,128)(2,1)S(1)}, u32[]{:S(2)}, u32[]{:S(2)}) collective-permute-start(bf16[2,1,96,256]{3,2,0,1:T(8,128)(2,1)S(1)} %get-tuple-element.56), channel_id=1, source_target_pairs={{0,1},{1,0},{2,3},{3,2},{4,5},{5,4},{6,7},{7,6},{8,9},{9,8},{10,11... | collective-permute-start | bytes 294920 | tf_op jit(solution)/shard_map/ppermute | solution.py:97
  151.4 4.7 %collective-permute-start.1 = (bf16[2,1,96,256]{3,2,0,1:T(8,128)(2,1)S(1)}, bf16[2,1,96,256]{3,2,0,1:T(8,128)(2,1)S(1)}, u32[]{:S(2)}, u32[]{:S(2)}) collective-permute-start(bf16[2,1,96,256]{3,2,0,1:T(8,128)(2,1)S(1)} %get-tuple-element.55), channel_id=1, source_target_pairs={{0,2},{1,3},{2,0},{3,1},{4,6},{5,7},{6,4},{7,5},{8,10},{9,11},{10,... | collective-permute-start | bytes 294920 | tf_op jit(solution)/shard_map/ppermute | solution.py:97
  156.1 5.3 %collective-permute-start.2 = (bf16[2,1,96,256]{3,2,0,1:T(8,128)(2,1)S(1)}, bf16[2,1,96,256]{3,2,0,1:T(8,128)(2,1)S(1)}, u32[]{:S(2)}, u32[]{:S(2)}) collective-permute-start(bf16[2,1,96,256]{3,2,0,1:T(8,128)(2,1)S(1)} %get-tuple-element.54), channel_id=1, source_target_pairs={{0,3},{1,2},{2,1},{3,0},{4,7},{5,6},{6,5},{7,4},{8,11},{9,10},{10,... | collective-permute-start | bytes 294920 | tf_op jit(solution)/shard_map/ppermute | solution.py:97
  161.4 5.1 %collective-permute-start.3 = (bf16[2,1,96,256]{3,2,0,1:T(8,128)(2,1)S(1)}, bf16[2,1,96,256]{3,2,0,1:T(8,128)(2,1)S(1)}, u32[]{:S(2)}, u32[]{:S(2)}) collective-permute-start(bf16[2,1,96,256]{3,2,0,1:T(8,128)(2,1)S(1)} %get-tuple-element.53), channel_id=1, source_target_pairs={{0,4},{1,5},{2,6},{3,7},{4,0},{5,1},{6,2},{7,3},{8,12},{9,13},{10,... | collective-permute-start | bytes 294920 | tf_op jit(solution)/shard_map/ppermute | solution.py:97
  166.5 5.5 %collective-permute-start.4 = (bf16[2,1,96,256]{3,2,0,1:T(8,128)(2,1)S(1)}, bf16[2,1,96,256]{3,2,0,1:T(8,128)(2,1)S(1)}, u32[]{:S(2)}, u32[]{:S(2)}) collective-permute-start(bf16[2,1,96,256]{3,2,0,1:T(8,128)(2,1)S(1)} %get-tuple-element.52), channel_id=1, source_target_pairs={{0,5},{1,4},{2,7},{3,6},{4,1},{5,0},{6,3},{7,2},{8,13},{9,12},{10,... | collective-permute-start | bytes 294920 | tf_op jit(solution)/shard_map/ppermute | solution.py:97
  172.0 4.9 %collective-permute-start.5 = (bf16[2,1,96,256]{3,2,0,1:T(8,128)(2,1)S(1)}, bf16[2,1,96,256]{3,2,0,1:T(8,128)(2,1)S(1)}, u32[]{:S(2)}, u32[]{:S(2)}) collective-permute-start(bf16[2,1,96,256]{3,2,0,1:T(8,128)(2,1)S(1)} %get-tuple-element.51), channel_id=1, source_target_pairs={{0,6},{1,7},{2,4},{3,5},{4,2},{5,3},{6,0},{7,1},{8,14},{9,15},{10,... | collective-permute-start | bytes 294920 | tf_op jit(solution)/shard_map/ppermute | solution.py:97
  176.9 5.8 %collective-permute-start.6 = (bf16[2,1,96,256]{3,2,0,1:T(8,128)(2,1)S(1)}, bf16[2,1,96,256]{3,2,0,1:T(8,128)(2,1)S(1)}, u32[]{:S(2)}, u32[]{:S(2)}) collective-permute-start(bf16[2,1,96,256]{3,2,0,1:T(8,128)(2,1)S(1)} %get-tuple-element.50), channel_id=1, source_target_pairs={{0,7},{1,6},{2,5},{3,4},{4,3},{5,2},{6,1},{7,0},{8,15},{9,14},{10,... | collective-permute-start | bytes 294920 | tf_op jit(solution)/shard_map/ppermute | solution.py:97
  182.7 4.5 %collective-permute-start.7 = (bf16[2,1,96,256]{3,2,0,1:T(8,128)(2,1)S(1)}, bf16[2,1,96,256]{3,2,0,1:T(8,128)(2,1)S(1)}, u32[]{:S(2)}, u32[]{:S(2)}) collective-permute-start(bf16[2,1,96,256]{3,2,0,1:T(8,128)(2,1)S(1)} %get-tuple-element.49), channel_id=1, source_target_pairs={{0,8},{1,9},{2,10},{3,11},{4,12},{5,13},{6,14},{7,15},{8,0},{9,1},... | collective-permute-start | bytes 294920 | tf_op jit(solution)/shard_map/ppermute | solution.py:97
  187.1 8.0 %collective-permute-start.8 = (bf16[2,1,96,256]{3,2,0,1:T(8,128)(2,1)S(1)}, bf16[2,1,96,256]{3,2,0,1:T(8,128)(2,1)S(1)}, u32[]{:S(2)}, u32[]{:S(2)}) collective-permute-start(bf16[2,1,96,256]{3,2,0,1:T(8,128)(2,1)S(1)} %get-tuple-element.48), channel_id=1, source_target_pairs={{0,9},{1,8},{2,11},{3,10},{4,13},{5,12},{6,15},{7,14},{8,1},{9,0},... | collective-permute-start | bytes 294920 | tf_op jit(solution)/shard_map/ppermute | solution.py:97
  195.2 6.1 %collective-permute-start.9 = (bf16[2,1,96,256]{3,2,0,1:T(8,128)(2,1)S(1)}, bf16[2,1,96,256]{3,2,0,1:T(8,128)(2,1)S(1)}, u32[]{:S(2)}, u32[]{:S(2)}) collective-permute-start(bf16[2,1,96,256]{3,2,0,1:T(8,128)(2,1)S(1)} %get-tuple-element.47), channel_id=1, source_target_pairs={{0,10},{1,11},{2,8},{3,9},{4,14},{5,15},{6,12},{7,13},{8,2},{9,3},... | collective-permute-start | bytes 294920 | tf_op jit(solution)/shard_map/ppermute | solution.py:97
  201.3 7.5 %collective-permute-start.10 = (bf16[2,1,96,256]{3,2,0,1:T(8,128)(2,1)S(1)}, bf16[2,1,96,256]{3,2,0,1:T(8,128)(2,1)S(1)}, u32[]{:S(2)}, u32[]{:S(2)}) collective-permute-start(bf16[2,1,96,256]{3,2,0,1:T(8,128)(2,1)S(1)} %get-tuple-element.46), channel_id=1, source_target_pairs={{0,11},{1,10},{2,9},{3,8},{4,15},{5,14},{6,13},{7,12},{8,3},{9,2},... | collective-permute-start | bytes 294920 | tf_op jit(solution)/shard_map/ppermute | solution.py:97
  208.8 76.7 %collective-permute-start.29 = (bf16[2,1,96,256]{3,2,0,1:T(8,128)(2,1)S(1)}, bf16[2,1,96,256]{3,2,0,1:T(8,128)(2,1)S(1)}, u32[]{:S(2)}, u32[]{:S(2)}) collective-permute-start(bf16[2,1,96,256]{3,2,0,1:T(8,128)(2,1)S(1)} %get-tuple-element.27), channel_id=1, source_target_pairs={{0,15},{1,14},{2,13},{3,12},{4,11},{5,10},{6,9},{7,8},{8,7},{9,6},... | collective-permute-start | bytes 294920 | tf_op jit(solution)/shard_map/ppermute | solution.py:97
  211.6 68.5 %collective-permute-start.28 = (bf16[2,1,96,256]{3,2,0,1:T(8,128)(2,1)S(1)}, bf16[2,1,96,256]{3,2,0,1:T(8,128)(2,1)S(1)}, u32[]{:S(2)}, u32[]{:S(2)}) collective-permute-start(bf16[2,1,96,256]{3,2,0,1:T(8,128)(2,1)S(1)} %get-tuple-element.28), channel_id=1, source_target_pairs={{0,14},{1,15},{2,12},{3,13},{4,10},{5,11},{6,8},{7,9},{8,6},{9,7},... | collective-permute-start | bytes 294920 | tf_op jit(solution)/shard_map/ppermute | solution.py:97
  212.2 67.2 %collective-permute-start.27 = (bf16[2,1,96,256]{3,2,0,1:T(8,128)(2,1)S(1)}, bf16[2,1,96,256]{3,2,0,1:T(8,128)(2,1)S(1)}, u32[]{:S(2)}, u32[]{:S(2)}) collective-permute-start(bf16[2,1,96,256]{3,2,0,1:T(8,128)(2,1)S(1)} %get-tuple-element.29), channel_id=1, source_target_pairs={{0,13},{1,12},{2,15},{3,14},{4,9},{5,8},{6,11},{7,10},{8,5},{9,4},... | collective-permute-start | bytes 294920 | tf_op jit(solution)/shard_map/ppermute | solution.py:97
  214.7 64.0 %collective-permute-start.26 = (bf16[2,1,96,256]{3,2,0,1:T(8,128)(2,1)S(1)}, bf16[2,1,96,256]{3,2,0,1:T(8,128)(2,1)S(1)}, u32[]{:S(2)}, u32[]{:S(2)}) collective-permute-start(bf16[2,1,96,256]{3,2,0,1:T(8,128)(2,1)S(1)} %get-tuple-element.30), channel_id=1, source_target_pairs={{0,12},{1,13},{2,14},{3,15},{4,8},{5,9},{6,10},{7,11},{8,4},{9,5},... | collective-permute-start | bytes 294920 | tf_op jit(solution)/shard_map/ppermute | solution.py:97
  215.8 1.3 collective-permute-start.15
  217.1 4.8 %collective-permute-start.16 = (bf16[2,1,96,256]{3,2,0,1:T(8,128)(2,1)S(1)}, bf16[2,1,96,256]{3,2,0,1:T(8,128)(2,1)S(1)}, u32[]{:S(2)}, u32[]{:S(2)}) collective-permute-start(bf16[2,1,96,256]{3,2,0,1:T(8,128)(2,1)S(1)} %get-tuple-element.40), channel_id=1, source_target_pairs={{0,2},{1,3},{2,0},{3,1},{4,6},{5,7},{6,4},{7,5},{8,10},{9,11},{10,... | collective-permute-start | bytes 294920 | tf_op jit(solution)/shard_map/ppermute | solution.py:97
  221.9 5.3 %collective-permute-start.17 = (bf16[2,1,96,256]{3,2,0,1:T(8,128)(2,1)S(1)}, bf16[2,1,96,256]{3,2,0,1:T(8,128)(2,1)S(1)}, u32[]{:S(2)}, u32[]{:S(2)}) collective-permute-start(bf16[2,1,96,256]{3,2,0,1:T(8,128)(2,1)S(1)} %get-tuple-element.39), channel_id=1, source_target_pairs={{0,3},{1,2},{2,1},{3,0},{4,7},{5,6},{6,5},{7,4},{8,11},{9,10},{10,... | collective-permute-start | bytes 294920 | tf_op jit(solution)/shard_map/ppermute | solution.py:97
  227.1 8.1 %collective-permute-start.18 = (bf16[2,1,96,256]{3,2,0,1:T(8,128)(2,1)S(1)}, bf16[2,1,96,256]{3,2,0,1:T(8,128)(2,1)S(1)}, u32[]{:S(2)}, u32[]{:S(2)}) collective-permute-start(bf16[2,1,96,256]{3,2,0,1:T(8,128)(2,1)S(1)} %get-tuple-element.38), channel_id=1, source_target_pairs={{0,4},{1,5},{2,6},{3,7},{4,0},{5,1},{6,2},{7,3},{8,12},{9,13},{10,... | collective-permute-start | bytes 294920 | tf_op jit(solution)/shard_map/ppermute | solution.py:97
  235.2 5.8 %collective-permute-start.19 = (bf16[2,1,96,256]{3,2,0,1:T(8,128)(2,1)S(1)}, bf16[2,1,96,256]{3,2,0,1:T(8,128)(2,1)S(1)}, u32[]{:S(2)}, u32[]{:S(2)}) collective-permute-start(bf16[2,1,96,256]{3,2,0,1:T(8,128)(2,1)S(1)} %get-tuple-element.37), channel_id=1, source_target_pairs={{0,5},{1,4},{2,7},{3,6},{4,1},{5,0},{6,3},{7,2},{8,13},{9,12},{10,... | collective-permute-start | bytes 294920 | tf_op jit(solution)/shard_map/ppermute | solution.py:97
  241.0 5.1 %collective-permute-start.20 = (bf16[2,1,96,256]{3,2,0,1:T(8,128)(2,1)S(1)}, bf16[2,1,96,256]{3,2,0,1:T(8,128)(2,1)S(1)}, u32[]{:S(2)}, u32[]{:S(2)}) collective-permute-start(bf16[2,1,96,256]{3,2,0,1:T(8,128)(2,1)S(1)} %get-tuple-element.36), channel_id=1, source_target_pairs={{0,6},{1,7},{2,4},{3,5},{4,2},{5,3},{6,0},{7,1},{8,14},{9,15},{10,... | collective-permute-start | bytes 294920 | tf_op jit(solution)/shard_map/ppermute | solution.py:97
  246.1 6.0 %collective-permute-start.21 = (bf16[2,1,96,256]{3,2,0,1:T(8,128)(2,1)S(1)}, bf16[2,1,96,256]{3,2,0,1:T(8,128)(2,1)S(1)}, u32[]{:S(2)}, u32[]{:S(2)}) collective-permute-start(bf16[2,1,96,256]{3,2,0,1:T(8,128)(2,1)S(1)} %get-tuple-element.35), channel_id=1, source_target_pairs={{0,7},{1,6},{2,5},{3,4},{4,3},{5,2},{6,1},{7,0},{8,15},{9,14},{10,... | collective-permute-start | bytes 294920 | tf_op jit(solution)/shard_map/ppermute | solution.py:97
  252.1 4.4 %collective-permute-start.22 = (bf16[2,1,96,256]{3,2,0,1:T(8,128)(2,1)S(1)}, bf16[2,1,96,256]{3,2,0,1:T(8,128)(2,1)S(1)}, u32[]{:S(2)}, u32[]{:S(2)}) collective-permute-start(bf16[2,1,96,256]{3,2,0,1:T(8,128)(2,1)S(1)} %get-tuple-element.34), channel_id=1, source_target_pairs={{0,8},{1,9},{2,10},{3,11},{4,12},{5,13},{6,14},{7,15},{8,0},{9,1},... | collective-permute-start | bytes 294920 | tf_op jit(solution)/shard_map/ppermute | solution.py:97
  256.6 7.2 %collective-permute-start.23 = (bf16[2,1,96,256]{3,2,0,1:T(8,128)(2,1)S(1)}, bf16[2,1,96,256]{3,2,0,1:T(8,128)(2,1)S(1)}, u32[]{:S(2)}, u32[]{:S(2)}) collective-permute-start(bf16[2,1,96,256]{3,2,0,1:T(8,128)(2,1)S(1)} %get-tuple-element.33), channel_id=1, source_target_pairs={{0,9},{1,8},{2,11},{3,10},{4,13},{5,12},{6,15},{7,14},{8,1},{9,0},... | collective-permute-start | bytes 294920 | tf_op jit(solution)/shard_map/ppermute | solution.py:97
  263.7 7.0 %collective-permute-start.24 = (bf16[2,1,96,256]{3,2,0,1:T(8,128)(2,1)S(1)}, bf16[2,1,96,256]{3,2,0,1:T(8,128)(2,1)S(1)}, u32[]{:S(2)}, u32[]{:S(2)}) collective-permute-start(bf16[2,1,96,256]{3,2,0,1:T(8,128)(2,1)S(1)} %get-tuple-element.32), channel_id=1, source_target_pairs={{0,10},{1,11},{2,8},{3,9},{4,14},{5,15},{6,12},{7,13},{8,2},{9,3},... | collective-permute-start | bytes 294920 | tf_op jit(solution)/shard_map/ppermute | solution.py:97
  270.7 7.4 %collective-permute-start.25 = (bf16[2,1,96,256]{3,2,0,1:T(8,128)(2,1)S(1)}, bf16[2,1,96,256]{3,2,0,1:T(8,128)(2,1)S(1)}, u32[]{:S(2)}, u32[]{:S(2)}) collective-permute-start(bf16[2,1,96,256]{3,2,0,1:T(8,128)(2,1)S(1)} %get-tuple-element.31), channel_id=1, source_target_pairs={{0,11},{1,10},{2,9},{3,8},{4,15},{5,14},{6,13},{7,12},{8,3},{9,2},... | collective-permute-start | bytes 294920 | tf_op jit(solution)/shard_map/ppermute | solution.py:97
